TPU v7x, 512 devices: a whole 4x8x8 slice. The times are simulated.
512 devices in a mesh: prompt: 32 (over x, y), sample: 16 (over z, core).
Axes of the slice: x: 4, y: 8, z: 8, core: 2. Of those that a mesh axis runs over, the one named last changes fastest.
Arguments:
- queries: bfloat16 [32, 16, 4, 8192], P('prompt', 'sample'), may hold values from -24 to 24
- new_kv: bfloat16 [32, 16, 4, 2, 1024], P('prompt', 'sample'), may hold values from -24 to 24
- suffix_kv: bfloat16 [32, 16, 256, 2, 1024], P('prompt', 'sample'), may hold values from -24 to 24
- suffix_len: int32 [32, 16], P('prompt', 'sample'), may hold values from 1 to 256, as said below
- prefix_head: bfloat16 [32, 2048, 2, 1024], P('prompt', 'sample'), may hold values from -24 to 24
- prefix_tail: bfloat16 [32, 2048, 2, 1024], P('prompt', 'sample'), may hold values from -24 to 24
- prefix_len: int32 [32], replicated, may hold values from 1024 to 4096, as said below
Outputs:
- attended: bfloat16 [32, 16, 4, 8192], P('prompt', 'sample')
Inputs may be any that keep to these rules, and one draw needn't show every extreme that they name: `suffix_len`: some sample has all 256 slots live and some only one. `prefix_len`: some prompt has all 4096 positions live and some only 1024.
All inputs are finite; a program needn't handle non-finite values.
Results may differ from a plain program's by a relative error of at most 0.001.
Values may be sent and summed in bfloat16 or wider, within the bound.
No kernel may reach another device: no remote copies, remote signals or barrier semaphores. Data moves between devices by JAX's collectives and lax.ppermute only.
A program may use at most 64 MiB of HBM per device.

v0:
```python
import jax
import jax.numpy as jnp
from jax import lax
from jax.sharding import PartitionSpec as P

QH = 64
KVH = 8
HEAD_SIZE = 128
NEG = -1e30


def from_behind(value, axis, steps):
    count = lax.axis_size(axis)
    pairs = [(source, (source + steps) % count) for source in range(count)]
    return lax.ppermute(value, axis, pairs)


def apply_weights(logit_scores, valid_mask, value_matrix, form):
    masked = jnp.where(valid_mask, logit_scores, NEG)
    maxima = jnp.max(masked, axis=-1)
    weights = jnp.where(valid_mask, jnp.exp(masked - maxima[..., None]), 0.0)
    totals = jnp.sum(weights, axis=-1)
    numerator = jnp.einsum(form, weights, value_matrix, precision=lax.Precision.HIGHEST)
    leading = numerator.shape[:2]
    return (
        numerator.reshape(leading + (QH, HEAD_SIZE)),
        maxima.reshape(leading + (QH,)),
        totals.reshape(leading + (QH,)),
    )


def prefix_terms(query_rows, pairs, start, length):
    sample_count, step_count = (query_rows.shape[0], query_rows.shape[1])
    block_len = pairs.shape[0]
    grouped_queries = query_rows.reshape(sample_count, step_count, KVH, QH // KVH, HEAD_SIZE)
    key_matrix = pairs[:, 0].reshape(block_len, KVH, HEAD_SIZE)
    value_matrix = pairs[:, 1].reshape(block_len, KVH, HEAD_SIZE).astype(jnp.float32)
    logit_scores = jnp.einsum(
        "rhlxf,vlf->rhlxv", grouped_queries, key_matrix, preferred_element_type=jnp.float32
    ) * HEAD_SIZE ** (-0.5)
    valid_mask = start + jnp.arange(block_len, dtype=jnp.int32) < length
    return apply_weights(logit_scores, valid_mask, value_matrix, "urpyj,jpi->urpyi")


def suffix_terms(query_rows, cache, fresh, length):
    sample_count, step_count = (query_rows.shape[0], query_rows.shape[1])
    slots = cache.shape[1]
    joined = jnp.concatenate([cache, fresh], axis=1)
    total_len = joined.shape[1]
    grouped_queries = query_rows.reshape(sample_count, step_count, KVH, QH // KVH, HEAD_SIZE)
    key_matrix = joined[:, :, 0].reshape(sample_count, total_len, KVH, HEAD_SIZE)
    value_matrix = (
        joined[:, :, 1].reshape(sample_count, total_len, KVH, HEAD_SIZE).astype(jnp.float32)
    )
    logit_scores = jnp.einsum(
        "stkgd,slkd->stkgl", grouped_queries, key_matrix, preferred_element_type=jnp.float32
    ) * HEAD_SIZE ** (-0.5)
    cache_live = jnp.arange(slots, dtype=jnp.int32)[None, :] < length[:, None]
    steps_live = (
        jnp.arange(step_count, dtype=jnp.int32)[None, :]
        <= jnp.arange(step_count, dtype=jnp.int32)[:, None]
    )
    valid_mask = jnp.concatenate(
        [
            jnp.broadcast_to(cache_live[:, None, :], (sample_count, step_count, slots)),
            steps_live[None],
        ],
        axis=2,
    )
    return apply_weights(
        logit_scores, valid_mask[:, :, None, None, :], value_matrix, "stkgl,slkd->stkgd"
    )


def join(former, latter):
    maxima = jnp.maximum(former[1], latter[1])
    scale_a = jnp.exp(former[1] - maxima)
    scale_b = jnp.exp(latter[1] - maxima)
    return (
        former[0] * scale_a[..., None] + latter[0] * scale_b[..., None],
        maxima,
        former[2] * scale_a + latter[2] * scale_b,
    )


def settle(stacked):
    maxima = jnp.max(stacked[1], axis=0)
    factors = jnp.exp(stacked[1] - maxima[None])
    return (
        jnp.sum(stacked[0] * factors[..., None], axis=0),
        maxima,
        jnp.sum(stacked[2] * factors, axis=0),
    )


def spread(partial_sums):
    return (
        lax.all_to_all(partial_sums[0][None], "sample", split_axis=1, concat_axis=0, tiled=True),
        lax.all_to_all(partial_sums[1][None], "sample", split_axis=1, concat_axis=0, tiled=True),
        lax.all_to_all(partial_sums[2][None], "sample", split_axis=1, concat_axis=0, tiled=True),
    )


def per_device(queries, new_kv, suffix_kv, suffix_len, prefix_head, prefix_tail, prefix_len):
    sample_count = lax.axis_size("sample")
    prompt_row = lax.axis_index("prompt")
    sample_slot = lax.axis_index("sample")
    block_len = prefix_head.shape[1]
    half_len = block_len * sample_count
    own_length = prefix_len[prompt_row]
    local_rows = queries[0]
    every_rows = lax.all_gather(queries, "sample", axis=1, tiled=True)[0]
    near_part = suffix_terms(local_rows, suffix_kv[0], new_kv[0], suffix_len[0])
    moved = from_behind(prefix_tail, "prompt", -1)
    own_part = prefix_terms(every_rows, prefix_head[0], sample_slot * block_len, own_length)
    tail_part = prefix_terms(every_rows, moved[0], half_len + sample_slot * block_len, own_length)
    result = join(settle(spread(join(own_part, tail_part))), near_part)
    attended = (result[0] / result[2][..., None]).astype(jnp.bfloat16)
    return attended.reshape(queries.shape)


def solution(mesh):
    in_specs = (
        P("prompt", "sample", None, None),
        P("prompt", "sample", None, None, None),
        P("prompt", "sample", None, None, None),
        P("prompt", "sample"),
        P("prompt", "sample", None, None),
        P("prompt", "sample", None, None),
        P(),
    )
    out_specs = P("prompt", "sample", None, None)
    return jax.shard_map(
        per_device, mesh=mesh, in_specs=in_specs, out_specs=out_specs, check_vma=False
    )
```

profile of v0, /device:TPU:1, one launch (start us, length us, event | category | flops | bytes accessed | tf_op | source)
XLA Modules:
  0.0 154.0 jit_solution(10899200841303403284)
XLA Ops:
  6.5 0.7 all-gather.2.cloned.1.call-update
  7.3 1.4 copy.107
  8.6 8.1 %collective-permute-start = (bf16[1,128,2,1024]{1,3,2,0:T(8,128)(2,1)S(1)}, bf16[1,128,2,1024]{1,3,2,0:T(8,128)(2,1)S(1)}, u32[]{:S(2)}, u32[]{:S(2)}) collective-permute-start(bf16[1,128,2,1024]{1,3,2,0:T(8,128)(2,1)S(1)} %copy.107), channel_id=1, source_target_pairs={{0,496},{16,0},{32,16},{48,32},{64,48},{80,64},{96,80},{112,96},{1... | collective-permute-start | bytes 1572872 | tf_op jit(solution)/shard_map/ppermute | solution.py:15
  16.8 1.4 copy.98
  18.2 0.6 dynamic_slice.3
  18.8 0.7 add_compare_fusion.1
  19.4 0.7 add_compare_fusion
  20.1 7.2 %collective-permute-done = bf16[1,128,2,1024]{1,3,2,0:T(8,128)(2,1)S(1)} collective-permute-done((bf16[1,128,2,1024]{1,3,2,0:T(8,128)(2,1)S(1)}, bf16[1,128,2,1024]{1,3,2,0:T(8,128)(2,1)S(1)}, u32[]{:S(2)}, u32[]{:S(2)}) %collective-permute-start) | collective-permute-done | bytes 524320 | tf_op jit(solution)/shard_map/ppermute | solution.py:15
  27.4 30.0 %all-gather.2.cloned.1.call-done = bf16[1,16,4,8192]{3,2,0,1:T(4,128)(2,1)} async-done(((bf16[1,1,4,8192]{3,2,0,1:T(4,128)(2,1)}), bf16[1,16,4,8192]{3,2,0,1:T(4,128)(2,1)}) %all-gather.2.cloned.1.call-update) | async-done | bytes 1048592 | tf_op jit(solution)/shard_map/all_gather | solution.py:112
  57.4 2.1 %reshape.433 = bf16[16,4,8,8,128]{4,3,2,1,0:T(8,128)(2,1)S(1)} reshape(bf16[1,16,4,8192]{3,2,0,1:T(4,128)(2,1)} %all-gather.2.cloned.1.call-done) | data formatting | bytes 2097152 | tf_op jit(solution)/shard_map/reshape;squeeze | solution.py:35
  59.5 1.0 bitcast_reduce_fusion
  60.6 1.0 bitcast_reduce_fusion.1
  61.6 3.3 %fusion.47 = (f32[16,4,8,8]{0,3,1,2:T(8,128)S(1)}, f32[16,4,8,8,128]{4,0,3,1,2:T(8,128)}, f32[16,4,8,8]{0,3,1,2:T(8,128)S(1)}, f32[16,4,8,8,128]{4,0,3,1,2:T(8,128)}) fusion(f32[16,4,8,8]{0,3,1,2:T(8,128)S(1)} %get-tuple-element.26, f32[8,128,16,4,8]{1,2,4,3,0:T(8,128)S(1)} %get-tuple-element.27, pred[128]{0:T(512)(128)(4,1)S(1)} %add_compare_fusion.1, ...), kind=kLoop, calls=%fused_computation.79 | loop fusion | flops 5234688 | bytes 8454400 | tf_op jit(solution)/shard_map/reduce_sum | solution.py:22
  64.9 0.1 fusion.31
  64.9 0.1 copy.123
  65.0 0.7 reshape.437
  65.7 4.5 %all-to-all-start.1 = ((f32[16,1,256]{2,1,0:T(1,128)}), f32[16,1,256]{2,1,0:T(1,128)S(1)}, u32[]{:S(2)}, u32[]{:S(2)}) async-start(f32[16,1,256]{2,1,0:T(1,128)} %reshape.437), calls=%async_computation.1 | async-start | bytes 32768 | tf_op jit(solution)/shard_map/all_to_all | solution.py:99
  70.2 0.1 copy.112
  70.3 0.1 copy.113
  70.4 3.4 %fusion.11 = f32[16,4,8,8,128]{4,3,1,0,2:T(8,128)S(1)} fusion(bf16[128,8,128,1,1]{0,2,4,3,1:T(8,128)(2,1)S(1)} %bitcast.166, f32[16,4,8,8,128]{4,0,3,1,2:T(8,128)} %get-tuple-element.11), kind=kOutput, calls=%fused_computation.20 | convolution fusion | flops 805306368 | bytes 4456448 | tf_op jit(solution)/shard_map/urpyj,jpi->urpyi/dot_general | solution.py:23
  73.8 3.1 %fusion.14 = f32[16,4,8,8,128]{4,3,1,0,2:T(8,128)} fusion(bf16[128,8,128,1,1]{0,2,4,3,1:T(8,128)(2,1)S(1)} %bitcast.167, f32[16,4,8,8,128]{4,0,3,1,2:T(8,128)S(1)} %copy-done), kind=kOutput, calls=%fused_computation.21 | convolution fusion | flops 805306368 | bytes 4456448 | tf_op jit(solution)/shard_map/urpyj,jpi->urpyi/dot_general | solution.py:23
  76.9 0.1 copy.131
  77.0 0.7 reshape.439
  77.7 7.2 %all-to-all-start.2 = ((f32[16,1,256]{2,1,0:T(1,128)}), f32[16,1,256]{2,1,0:T(1,128)S(1)}, u32[]{:S(2)}, u32[]{:S(2)}) async-start(f32[16,1,256]{2,1,0:T(1,128)} %reshape.439), calls=%async_computation.2 | async-start | bytes 32768 | tf_op jit(solution)/shard_map/all_to_all | solution.py:100
  84.9 3.4 %fusion.2 = f32[1,16,4,64,128]{4,3,2,0,1:T(8,128)} fusion(f32[16,4,8,8,128]{4,3,1,0,2:T(8,128)} %fusion.14, f32[16,4,8,8,128]{4,3,1,0,2:T(8,128)S(1)} %fusion.11, f32[16,4,64]{2,1,0:T(4,128)S(1)} %copy.119, f32[16,4,64]{2,1,0:T(4,128)S(1)} %copy.114), kind=kLoop, calls=%fused_computation.4 | loop fusion | flops 1572864 | bytes 6324224 | tf_op jit(solution)/shard_map/add | solution.py:80
  88.4 3.9 %all-to-all-done.2 = f32[16,1,256]{2,1,0:T(1,128)S(1)} async-done(((f32[16,1,256]{2,1,0:T(1,128)}), f32[16,1,256]{2,1,0:T(1,128)S(1)}, u32[]{:S(2)}, u32[]{:S(2)}) %all-to-all-start.2) | async-done | bytes 16416 | tf_op jit(solution)/shard_map/all_to_all | solution.py:100
  92.3 3.9 %all-to-all-start = ((f32[1,16,4,64,128]{4,3,2,0,1:T(8,128)}), f32[1,16,4,64,128]{4,3,2,0,1:T(8,128)S(1)}, u32[]{:S(2)}, u32[]{:S(2)}) async-start(f32[1,16,4,64,128]{4,3,2,0,1:T(8,128)} %fusion.2), calls=%async_computation | async-start | bytes 4194304 | tf_op jit(solution)/shard_map/all_to_all | solution.py:98
  96.8 0.0 copy-start.1
  96.8 12.8 %fusion.19 = (bf16[260,1024]{1,0:T(8,128)(2,1)S(1)}, bf16[260,1024]{1,0:T(8,128)(2,1)S(1)}) fusion(bf16[1,4,2,1024]{3,2,1,0:T(2,128)(2,1)S(1)} %bitcast.181, bf16[1,256,2,1024]{3,2,1,0:T(2,128)(2,1)} %bitcast.165), kind=kLoop, calls=%fused_computation.28 | loop fusion | flops 2129920 | bytes 2129920 | tf_op jit(solution)/shard_map/slice | solution.py:53
  109.6 0.1 copy.155
  109.8 0.4 fusion.53
  110.2 0.2 fusion.27
  110.5 0.1 reshape.426
  110.6 0.1 reshape.420
  110.6 0.1 copy.157
  110.8 0.5 convolution_bitcast_fusion
  111.4 0.5 broadcast.97
  111.9 0.7 reduce.10
  112.6 0.1 reshape.438
  112.6 0.7 reduce.11
  113.3 0.1 reshape.440
  113.5 31.7 %all-to-all-done = f32[1,16,4,64,128]{4,3,2,0,1:T(8,128)S(1)} async-done(((f32[1,16,4,64,128]{4,3,2,0,1:T(8,128)}), f32[1,16,4,64,128]{4,3,2,0,1:T(8,128)S(1)}, u32[]{:S(2)}, u32[]{:S(2)}) %all-to-all-start) | async-done | bytes 2097184 | tf_op jit(solution)/shard_map/all_to_all | solution.py:98
  145.2 0.7 fusion
  145.9 0.1 broadcast_multiply_fusion
  146.0 0.1 mul.174
  146.1 0.1 div.19
  146.2 0.2 fusion.34
  146.4 0.7 copy.133
  (29 shorter events, 0.4 us)
Async XLA Ops:
  6.5 11.6 %copy-start.3 = (s32[32]{0:T(128)S(1)}, s32[32]{0:T(128)}, u32[]{:S(2)}) copy-start(s32[32]{0:T(128)} %param.13) | copy-start | bytes 388
  6.5 50.8 %all-gather.2.cloned.1.call-start = ((), (), s32[]{:S(2)}) async-start(), calls=%async_computation.3 | async-start | bytes 1114112 | tf_op jit(solution)/shard_map/all_gather | solution.py:112
  8.6 18.7 %collective-permute-start = (bf16[1,128,2,1024]{1,3,2,0:T(8,128)(2,1)S(1)}, bf16[1,128,2,1024]{1,3,2,0:T(8,128)(2,1)S(1)}, u32[]{:S(2)}, u32[]{:S(2)}) collective-permute-start(bf16[1,128,2,1024]{1,3,2,0:T(8,128)(2,1)S(1)} %copy.107), channel_id=1, source_target_pairs={{0,496},{16,0},{32,16},{48,32},{64,48},{80,64},{96,80},{112,96},{1... | collective-permute-start | bytes 1572872 | tf_op jit(solution)/shard_map/ppermute | solution.py:15
  65.7 12.0 %all-to-all-start.1 = ((f32[16,1,256]{2,1,0:T(1,128)}), f32[16,1,256]{2,1,0:T(1,128)S(1)}, u32[]{:S(2)}, u32[]{:S(2)}) async-start(f32[16,1,256]{2,1,0:T(1,128)} %reshape.437), calls=%async_computation.1 | async-start | bytes 32768 | tf_op jit(solution)/shard_map/all_to_all | solution.py:99
  70.4 3.4 %copy-start = (f32[16,4,8,8,128]{4,0,3,1,2:T(8,128)S(1)}, f32[16,4,8,8,128]{4,0,3,1,2:T(8,128)}, u32[]{:S(2)}) copy-start(f32[16,4,8,8,128]{4,0,3,1,2:T(8,128)} %get-tuple-element.29) | copy-start | bytes 6291460
  77.7 14.6 %all-to-all-start.2 = ((f32[16,1,256]{2,1,0:T(1,128)}), f32[16,1,256]{2,1,0:T(1,128)S(1)}, u32[]{:S(2)}, u32[]{:S(2)}) async-start(f32[16,1,256]{2,1,0:T(1,128)} %reshape.439), calls=%async_computation.2 | async-start | bytes 32768 | tf_op jit(solution)/shard_map/all_to_all | solution.py:100
  88.4 8.4 %copy-start.2 = (bf16[1,1,4,2,1024]{4,3,2,1,0:T(2,128)(2,1)S(1)}, bf16[1,1,4,2,1024]{4,3,2,1,0:T(2,128)(2,1)}, u32[]{:S(2)}) copy-start(bf16[1,1,4,2,1024]{4,3,2,1,0:T(2,128)(2,1)} %param.8) | copy-start | bytes 49156
  92.3 52.9 %all-to-all-start = ((f32[1,16,4,64,128]{4,3,2,0,1:T(8,128)}), f32[1,16,4,64,128]{4,3,2,0,1:T(8,128)S(1)}, u32[]{:S(2)}, u32[]{:S(2)}) async-start(f32[1,16,4,64,128]{4,3,2,0,1:T(8,128)} %fusion.2), calls=%async_computation | async-start | bytes 4194304 | tf_op jit(solution)/shard_map/all_to_all | solution.py:98
  96.8 13.0 %copy-start.1 = (bf16[1,1,4,8192]{3,2,1,0:T(4,128)(2,1)S(1)}, bf16[1,1,4,8192]{3,2,1,0:T(4,128)(2,1)}, u32[]{:S(2)}) copy-start(bf16[1,1,4,8192]{3,2,1,0:T(4,128)(2,1)} %param.7) | copy-start | bytes 196612
Sparse Core Ops, SparseCore 0:
  9.5 47.8 all-gather.1
where the time goes:
time: 154 us
  waiting for transfers between devices  73.5 us (48%)
  starting transfers between devices  23.7 us (15%)
  other arithmetic  23.6 us (15%)
  between operations  14.4 us (9%)
  matrix products  9.42 us (6%)
  local copies, waits for them, and re-layouts  9.41 us (6%)
    all_to_all x1, waiting for transfers between devices, spread(): lax.all_to_all(partial_sums[0][None], 'sample', split_axis=1, concat_axis...  31.7 us
    all_gather x1, waiting for transfers between devices, per_device(): every_rows = lax.all_gather(queries, 'sample', axis=1, tiled=True)[0]  30 us
    slice x1, other arithmetic, suffix_terms(): joined[:, :, 1].reshape(sample_count, total_len, KVH, HEAD_SIZE)  12.8 us
    ppermute x1, starting transfers between devices, from_behind(): return lax.ppermute(value, axis, pairs)  8.12 us
    all_to_all x1, starting transfers between devices, spread(): lax.all_to_all(partial_sums[2][None], 'sample', split_axis=1, concat_axis...  7.22 us
    ppermute x1, waiting for transfers between devices, from_behind(): return lax.ppermute(value, axis, pairs)  7.22 us
    dot_general x3, matrix products, apply_weights(): jnp.einsum(form, weights, value_matrix, precision=lax.Precision.HIGHEST)  7.01 us
    unnamed x16, local copies, waits for them, and re-layouts  4.55 us
  transfers between devices with their start and end apart: 5, of which 4 were waited for; matrix products, arithmetic and copies ran while one was open for 21% of the time, Pallas kernels for 0%

commit v1 on v0

--- a/solution.py
+++ b/solution.py
@@ -109,7 +109,9 @@
     half_len = block_len * sample_count
     own_length = prefix_len[prompt_row]
     local_rows = queries[0]
-    every_rows = lax.all_gather(queries, "sample", axis=1, tiled=True)[0]
+    every_rows = jnp.concatenate(
+        lax.all_to_all(jnp.stack([queries] * lax.axis_size("sample")), "sample", 0, 0), axis=1
+    )[0]
     near_part = suffix_terms(local_rows, suffix_kv[0], new_kv[0], suffix_len[0])
     moved = from_behind(prefix_tail, "prompt", -1)
     own_part = prefix_terms(every_rows, prefix_head[0], sample_slot * block_len, own_length)

time: 154 us -> 131 us (0.85)
  waiting for transfers between devices: 73.5 us -> 51.8 us
  between operations: 14.4 us -> 0.98 us
  starting transfers between devices: 23.7 us -> 33.9 us
    all_gather x1 -> x0, waiting for transfers between devices: 30 us -> none  [per_device(): every_rows = lax.all_gather(queries, 'sample', axis=1, tiled=True)[0]]
    all_to_all x0 -> x1, starting transfers between devices: none -> 12 us  [per_device(): lax.all_to_all(jnp.stack([queries] * lax.axis_size('sample')), 'sample',...]
    all_to_all x0 -> x1, waiting for transfers between devices: none -> 7.12 us  [per_device(): lax.all_to_all(jnp.stack([queries] * lax.axis_size('sample')), 'sample',...]
    another operation x2 -> x3, local copies, waits for them, and re-layouts: 0.07 us -> 2.4 us  [the longest x1 2.32 us: per_device(): jnp.stack([queries] * lax.axis_size('sample'))]
    ppermute x1, waiting for transfers between devices: 7.22 us -> 9.04 us  [from_behind(): return lax.ppermute(value, axis, pairs)]
    unnamed x16 -> x22, local copies, waits for them, and re-layouts: 4.55 us -> 3.53 us
  transfers between devices with their start and end apart: 5 -> 5, of which waited for: 4 -> 4; matrix products, arithmetic and copies ran while one was open for 21% -> 24% of each run, Pallas kernels for 0% -> 0%
where the time goes in v1:
time: 131 us; the launch traced here: 130 us
  waiting for transfers between devices  51.8 us (40%)
  starting transfers between devices  33.9 us (26%)
  other arithmetic  23.6 us (18%)
  local copies, waits for them, and re-layouts  10.4 us (8%)
  matrix products  9.42 us (7%)
    all_to_all x1, waiting for transfers between devices, spread(): lax.all_to_all(partial_sums[0][None], 'sample', split_axis=1, concat_axis...  31.7 us
    slice x1, other arithmetic, suffix_terms(): joined[:, :, 1].reshape(sample_count, total_len, KVH, HEAD_SIZE)  12.7 us
    all_to_all x1, starting transfers between devices, per_device(): lax.all_to_all(jnp.stack([queries] * lax.axis_size('sample')), 'sample',...  12 us
    ppermute x1, waiting for transfers between devices, from_behind(): return lax.ppermute(value, axis, pairs)  9.04 us
    ppermute x1, starting transfers between devices, from_behind(): return lax.ppermute(value, axis, pairs)  7.3 us
    all_to_all x1, starting transfers between devices, spread(): lax.all_to_all(partial_sums[2][None], 'sample', split_axis=1, concat_axis...  7.23 us
    all_to_all x1, waiting for transfers between devices, per_device(): lax.all_to_all(jnp.stack([queries] * lax.axis_size('sample')), 'sample',...  7.12 us
    dot_general x3, matrix products, apply_weights(): jnp.einsum(form, weights, value_matrix, precision=lax.Precision.HIGHEST)  7 us
  transfers between devices with their start and end apart: 5, of which 4 were waited for; matrix products, arithmetic and copies ran while one was open for 24% of the time, Pallas kernels for 0%

profile of v1, /device:TPU:1, one launch (start us, length us, event | category | flops | bytes accessed | tf_op | source)
XLA Modules:
  0.0 130.0 jit_solution(4202689732081595624)
XLA Ops:
  0.0 2.3 %stack.2 = bf16[16,1,1,4,8192]{4,3,2,1,0:T(4,128)(2,1)} broadcast(bf16[4,8192]{1,0:T(4,128)(2,1)} %bitcast.177), dimensions={3,4} | broadcast | bytes 1114112 | tf_op jit(solution)/shard_map/stack | solution.py:113
  2.3 12.0 %all-to-all-start = ((bf16[16,1,1,4,8192]{4,3,2,1,0:T(4,128)(2,1)}), bf16[16,1,1,4,8192]{4,3,2,1,0:T(4,128)(2,1)S(1)}, u32[]{:S(2)}, u32[]{:S(2)}) async-start(bf16[16,1,1,4,8192]{4,3,2,1,0:T(4,128)(2,1)} %stack.2), calls=%async_computation | async-start | bytes 2097152 | tf_op jit(solution)/shard_map/all_to_all | solution.py:113
  14.3 1.2 copy.103
  15.5 7.3 %collective-permute-start = (bf16[1,128,2,1024]{1,3,2,0:T(8,128)(2,1)}, bf16[1,128,2,1024]{1,3,2,0:T(8,128)(2,1)S(1)}, u32[]{:S(2)}, u32[]{:S(2)}) collective-permute-start(bf16[1,128,2,1024]{1,3,2,0:T(8,128)(2,1)} %copy.103), channel_id=1, source_target_pairs={{0,496},{16,0},{32,16},{48,32},{64,48},{80,64},{96,80},{112,96},{1... | collective-permute-start | bytes 1572872 | tf_op jit(solution)/shard_map/ppermute | solution.py:15
  22.8 0.5 copy.95
  23.4 0.6 dynamic_slice.3
  24.0 0.7 add_compare_fusion.1
  24.6 0.7 add_compare_fusion
  25.3 9.0 %collective-permute-done = bf16[1,128,2,1024]{1,3,2,0:T(8,128)(2,1)S(1)} collective-permute-done((bf16[1,128,2,1024]{1,3,2,0:T(8,128)(2,1)}, bf16[1,128,2,1024]{1,3,2,0:T(8,128)(2,1)S(1)}, u32[]{:S(2)}, u32[]{:S(2)}) %collective-permute-start) | collective-permute-done | bytes 524320 | tf_op jit(solution)/shard_map/ppermute | solution.py:15
  34.4 0.8 fusion.52
  35.1 7.1 %all-to-all-done = bf16[16,1,1,4,8192]{4,3,2,1,0:T(4,128)(2,1)S(1)} async-done(((bf16[16,1,1,4,8192]{4,3,2,1,0:T(4,128)(2,1)}), bf16[16,1,1,4,8192]{4,3,2,1,0:T(4,128)(2,1)S(1)}, u32[]{:S(2)}, u32[]{:S(2)}) %all-to-all-start) | async-done | bytes 1048608 | tf_op jit(solution)/shard_map/all_to_all | solution.py:113
  42.2 1.1 reshape.436
  43.3 1.0 bitcast_reduce_fusion
  44.4 1.0 bitcast_reduce_fusion.1
  45.4 3.3 %fusion.47 = (f32[16,4,8,8]{0,3,1,2:T(8,128)S(1)}, f32[16,4,8,8,128]{4,0,3,1,2:T(8,128)}, f32[16,4,8,8]{0,3,1,2:T(8,128)S(1)}, f32[16,4,8,8,128]{4,0,3,1,2:T(8,128)}) fusion(f32[16,4,8,8]{0,3,1,2:T(8,128)S(1)} %get-tuple-element.26, f32[8,128,16,4,8]{1,2,4,3,0:T(8,128)S(1)} %get-tuple-element.27, pred[128]{0:T(512)(128)(4,1)S(1)} %add_compare_fusion.1, ...), kind=kLoop, calls=%fused_computation.79 | loop fusion | flops 5234688 | bytes 8454400 | tf_op jit(solution)/shard_map/reduce_sum | solution.py:22
  48.8 0.1 copy.119
  48.8 0.7 reshape.440
  49.6 3.5 %all-to-all-start.2 = ((f32[16,1,256]{2,1,0:T(1,128)}), f32[16,1,256]{2,1,0:T(1,128)S(1)}, u32[]{:S(2)}, u32[]{:S(2)}) async-start(f32[16,1,256]{2,1,0:T(1,128)} %reshape.440), calls=%async_computation.2 | async-start | bytes 32768 | tf_op jit(solution)/shard_map/all_to_all | solution.py:99
  53.1 0.1 copy.108
  53.2 0.1 copy.109
  53.3 3.4 %fusion.11 = f32[16,4,8,8,128]{4,3,1,0,2:T(8,128)S(1)} fusion(bf16[128,8,128,1,1]{0,2,4,3,1:T(8,128)(2,1)S(1)} %bitcast.164, f32[16,4,8,8,128]{4,0,3,1,2:T(8,128)} %get-tuple-element.11), kind=kOutput, calls=%fused_computation.20 | convolution fusion | flops 805306368 | bytes 4456448 | tf_op jit(solution)/shard_map/urpyj,jpi->urpyi/dot_general | solution.py:23
  56.7 3.1 %fusion.14 = f32[16,4,8,8,128]{4,3,1,0,2:T(8,128)} fusion(bf16[128,8,128,1,1]{0,2,4,3,1:T(8,128)(2,1)S(1)} %bitcast.165, f32[16,4,8,8,128]{4,0,3,1,2:T(8,128)S(1)} %copy-done), kind=kOutput, calls=%fused_computation.21 | convolution fusion | flops 805306368 | bytes 4456448 | tf_op jit(solution)/shard_map/urpyj,jpi->urpyi/dot_general | solution.py:23
  59.8 0.1 copy.127
  59.9 0.7 reshape.442
  60.6 7.2 %all-to-all-start.3 = ((f32[16,1,256]{2,1,0:T(1,128)}), f32[16,1,256]{2,1,0:T(1,128)S(1)}, u32[]{:S(2)}, u32[]{:S(2)}) async-start(f32[16,1,256]{2,1,0:T(1,128)} %reshape.442), calls=%async_computation.3 | async-start | bytes 32768 | tf_op jit(solution)/shard_map/all_to_all | solution.py:100
  67.8 3.4 %fusion.2 = f32[1,16,4,64,128]{4,3,2,0,1:T(8,128)} fusion(f32[16,4,8,8,128]{4,3,1,0,2:T(8,128)} %fusion.14, f32[16,4,8,8,128]{4,3,1,0,2:T(8,128)S(1)} %fusion.11, f32[16,4,64]{2,1,0:T(4,128)S(1)} %copy.115, f32[16,4,64]{2,1,0:T(4,128)S(1)} %copy.110), kind=kLoop, calls=%fused_computation.4 | loop fusion | flops 1572864 | bytes 6324224 | tf_op jit(solution)/shard_map/add | solution.py:80
  71.3 3.9 %all-to-all-done.3 = f32[16,1,256]{2,1,0:T(1,128)S(1)} async-done(((f32[16,1,256]{2,1,0:T(1,128)}), f32[16,1,256]{2,1,0:T(1,128)S(1)}, u32[]{:S(2)}, u32[]{:S(2)}) %all-to-all-start.3) | async-done | bytes 16416 | tf_op jit(solution)/shard_map/all_to_all | solution.py:100
  75.2 3.9 %all-to-all-start.1 = ((f32[1,16,4,64,128]{4,3,2,0,1:T(8,128)}), f32[1,16,4,64,128]{4,3,2,0,1:T(8,128)S(1)}, u32[]{:S(2)}, u32[]{:S(2)}) async-start(f32[1,16,4,64,128]{4,3,2,0,1:T(8,128)} %fusion.2), calls=%async_computation.1 | async-start | bytes 4194304 | tf_op jit(solution)/shard_map/all_to_all | solution.py:98
  79.7 12.7 %fusion.19 = (bf16[260,1024]{1,0:T(8,128)(2,1)S(1)}, bf16[260,1024]{1,0:T(8,128)(2,1)S(1)}) fusion(bf16[1,4,2,1024]{3,2,1,0:T(2,128)(2,1)S(1)} %bitcast.179, bf16[1,256,2,1024]{3,2,1,0:T(2,128)(2,1)} %bitcast.163), kind=kLoop, calls=%fused_computation.28 | loop fusion | flops 2129920 | bytes 2129920 | tf_op jit(solution)/shard_map/slice | solution.py:53
  92.5 0.1 copy.151
  92.7 0.4 fusion.53
  93.1 0.2 fusion.27
  93.3 0.1 reshape.429
  93.4 0.1 reshape.423
  93.5 0.1 copy.153
  93.6 0.5 convolution_bitcast_fusion
  94.2 0.5 broadcast.100
  94.7 0.7 reduce.10
  95.4 0.1 reshape.441
  95.5 0.7 reduce.11
  96.2 0.1 reshape.443
  96.4 31.7 %all-to-all-done.1 = f32[1,16,4,64,128]{4,3,2,0,1:T(8,128)S(1)} async-done(((f32[1,16,4,64,128]{4,3,2,0,1:T(8,128)}), f32[1,16,4,64,128]{4,3,2,0,1:T(8,128)S(1)}, u32[]{:S(2)}, u32[]{:S(2)}) %all-to-all-start.1) | async-done | bytes 2097184 | tf_op jit(solution)/shard_map/all_to_all | solution.py:98
  128.1 0.7 fusion
  128.8 0.1 broadcast_multiply_fusion
  128.9 0.1 mul.174
  129.0 0.1 div.19
  129.1 0.2 fusion.34
  129.3 0.7 copy.129
  (35 shorter events, 0.4 us)
Async XLA Ops:
  0.0 14.3 %copy-start.1 = (bf16[1,128,2,1024]{3,2,1,0:T(2,128)(2,1)S(1)}, bf16[1,128,2,1024]{3,2,1,0:T(2,128)(2,1)}, u32[]{:S(2)}) copy-start(bf16[1,128,2,1024]{3,2,1,0:T(2,128)(2,1)} %param.12) | copy-start | bytes 1572868
  0.0 22.8 %copy-start.2 = (bf16[1,128,2,1024]{3,2,1,0:T(2,128)(2,1)S(1)}, bf16[1,128,2,1024]{3,2,1,0:T(2,128)(2,1)}, u32[]{:S(2)}) copy-start(bf16[1,128,2,1024]{3,2,1,0:T(2,128)(2,1)} %param.11) | copy-start | bytes 1572868
  2.3 21.0 %copy-start.6 = (s32[32]{0:T(128)S(1)}, s32[32]{0:T(128)}, u32[]{:S(2)}) copy-start(s32[32]{0:T(128)} %param.13) | copy-start | bytes 388
  2.3 39.9 %all-to-all-start = ((bf16[16,1,1,4,8192]{4,3,2,1,0:T(4,128)(2,1)}), bf16[16,1,1,4,8192]{4,3,2,1,0:T(4,128)(2,1)S(1)}, u32[]{:S(2)}, u32[]{:S(2)}) async-start(bf16[16,1,1,4,8192]{4,3,2,1,0:T(4,128)(2,1)} %stack.2), calls=%async_computation | async-start | bytes 2097152 | tf_op jit(solution)/shard_map/all_to_all | solution.py:113
  15.5 18.9 %collective-permute-start = (bf16[1,128,2,1024]{1,3,2,0:T(8,128)(2,1)}, bf16[1,128,2,1024]{1,3,2,0:T(8,128)(2,1)S(1)}, u32[]{:S(2)}, u32[]{:S(2)}) collective-permute-start(bf16[1,128,2,1024]{1,3,2,0:T(8,128)(2,1)} %copy.103), channel_id=1, source_target_pairs={{0,496},{16,0},{32,16},{48,32},{64,48},{80,64},{96,80},{112,96},{1... | collective-permute-start | bytes 1572872 | tf_op jit(solution)/shard_map/ppermute | solution.py:15
  35.1 8.2 %copy-start.3 = (bf16[128,1,1024]{0,2,1:T(8,128)(2,1)S(1)}, bf16[128,1,1024]{0,2,1:T(8,128)(2,1)}, u32[]{:S(2)}) copy-start(bf16[128,1,1024]{0,2,1:T(8,128)(2,1)} %get-tuple-element.17) | copy-start | bytes 786436
  49.6 11.0 %all-to-all-start.2 = ((f32[16,1,256]{2,1,0:T(1,128)}), f32[16,1,256]{2,1,0:T(1,128)S(1)}, u32[]{:S(2)}, u32[]{:S(2)}) async-start(f32[16,1,256]{2,1,0:T(1,128)} %reshape.440), calls=%async_computation.2 | async-start | bytes 32768 | tf_op jit(solution)/shard_map/all_to_all | solution.py:99
  53.3 3.4 %copy-start = (f32[16,4,8,8,128]{4,0,3,1,2:T(8,128)S(1)}, f32[16,4,8,8,128]{4,0,3,1,2:T(8,128)}, u32[]{:S(2)}) copy-start(f32[16,4,8,8,128]{4,0,3,1,2:T(8,128)} %get-tuple-element.29) | copy-start | bytes 6291460
  60.6 14.6 %all-to-all-start.3 = ((f32[16,1,256]{2,1,0:T(1,128)}), f32[16,1,256]{2,1,0:T(1,128)S(1)}, u32[]{:S(2)}, u32[]{:S(2)}) async-start(f32[16,1,256]{2,1,0:T(1,128)} %reshape.442), calls=%async_computation.3 | async-start | bytes 32768 | tf_op jit(solution)/shard_map/all_to_all | solution.py:100
  71.3 8.4 %copy-start.5 = (bf16[1,1,4,2,1024]{4,3,2,1,0:T(2,128)(2,1)S(1)}, bf16[1,1,4,2,1024]{4,3,2,1,0:T(2,128)(2,1)}, u32[]{:S(2)}) copy-start(bf16[1,1,4,2,1024]{4,3,2,1,0:T(2,128)(2,1)} %param.8) | copy-start | bytes 49156
  75.2 52.9 %all-to-all-start.1 = ((f32[1,16,4,64,128]{4,3,2,0,1:T(8,128)}), f32[1,16,4,64,128]{4,3,2,0,1:T(8,128)S(1)}, u32[]{:S(2)}, u32[]{:S(2)}) async-start(f32[1,16,4,64,128]{4,3,2,0,1:T(8,128)} %fusion.2), calls=%async_computation.1 | async-start | bytes 4194304 | tf_op jit(solution)/shard_map/all_to_all | solution.py:98
  79.7 12.9 %copy-start.4 = (bf16[1,1,4,8192]{3,2,1,0:T(4,128)(2,1)S(1)}, bf16[1,1,4,8192]{3,2,1,0:T(4,128)(2,1)}, u32[]{:S(2)}) copy-start(bf16[1,1,4,8192]{3,2,1,0:T(4,128)(2,1)} %param.7) | copy-start | bytes 196612
